TPU v7x, 256 devices: a whole 4x4x8 slice. The times are simulated.
256 devices in a mesh: seq: 32 (over x, z), exp: 8 (over y, core).
Axes of the slice: x: 4, y: 4, z: 8, core: 2. Of those that a mesh axis runs over, the one named last changes fastest.
Arguments:
- queries: bfloat16 [32768, 4096], P(('seq', 'exp')), may hold values from -1.75 to 1.75
- keys: bfloat16 [32768, 4096], P(('seq', 'exp')), may hold values from -1.75 to 1.75
- values: bfloat16 [32768, 4096], P(('seq', 'exp')), may hold values from -6 to 6
- out_grad: bfloat16 [32768, 4096], P(('seq', 'exp')), may hold values from -0.0625 to 0.0625
- log_decay: bfloat16 [32768, 32], P(('seq', 'exp')), may hold values from -0.7 to 0
Outputs:
- query_grad: bfloat16 [32768, 4096], P(('seq', 'exp'))
- key_grad: bfloat16 [32768, 4096], P(('seq', 'exp'))
- value_grad: bfloat16 [32768, 4096], P(('seq', 'exp'))
All inputs are finite; a program needn't handle non-finite values.
Results may differ from a plain program's by a relative error of at most 0.0095.
Values may be sent and summed in bfloat16 or wider, within the bound.
No kernel may reach another device: no remote copies, remote signals or barrier semaphores. Data moves between devices by JAX's collectives and lax.ppermute only.
A program may use at most 64 MiB of HBM per device.

v0:
```python
import jax
import jax.numpy as jnp
from jax import lax
from jax.sharding import Mesh
from jax.sharding import PartitionSpec as P

BLOCK = 128
SEQ = ("seq_0", "seq_1")
SEQ_EXP = ("seq_0", "seq_1", "exp")


def filled_with(x, identity):
    return jax.tree.map(
        lambda part, zero: jnp.zeros_like(part) + jnp.asarray(zero, part.dtype), x, identity
    )


def carried_in(x, axes, combine, identity, reverse):
    before = start = filled_with(x, identity)
    total = x
    for axis in reversed(axes):
        peers, here = (lax.axis_size(axis), lax.axis_index(axis))
        pieces = jax.tree.map(lambda part: lax.all_gather(part, axis), total)
        inside, total = (start, start)
        for k in reversed(range(peers)) if reverse else range(peers):
            passed = k > here if reverse else k < here
            total = combine(total, jax.tree.map(lambda part: part[k], pieces))
            inside = jax.tree.map(lambda new, old: jnp.where(passed, new, old), total, inside)
        before = combine(inside, before)
    return before


def widen(array):
    return array.astype(jnp.float32)


def halves(array):
    high = array.astype(jnp.bfloat16)
    low = (array - widen(high)).astype(jnp.bfloat16)
    return (high, low)


def product(form, first_op, second_op):
    return jnp.einsum(form, first_op, second_op, preferred_element_type=jnp.float32)


def split_left(form, wide_op, narrow_op):
    high, low = halves(wide_op)
    return product(form, high, narrow_op) + product(form, low, narrow_op)


def split_right(form, narrow_op, wide_op):
    high, low = halves(wide_op)
    return product(form, narrow_op, high) + product(form, narrow_op, low)


def link(earlier, later):
    return (earlier[0] + later[0], jnp.exp(later[0])[:, None, None] * earlier[1] + later[1])


def key_side(key_loc, value_loc, decay_loc):
    rows = key_loc.shape[0]
    heads = decay_loc.shape[1]
    width = key_loc.shape[1] // heads
    blocks = rows // BLOCK
    key_blk = key_loc.reshape(blocks, BLOCK, heads, width)
    value_blk = value_loc.reshape(blocks, BLOCK, heads, width)
    cumul = jnp.cumsum(widen(decay_loc).reshape(blocks, BLOCK, heads), axis=1)
    totals = cumul[:, -1, :]
    after = jnp.exp(totals[:, None, :] - cumul)
    contrib = split_left("nsha,nshb->nhab", after[..., None] * widen(key_blk), value_blk)

    def key_step(carry, item):
        state, logsum = carry
        total, piece = item
        return ((jnp.exp(total)[:, None, None] * state + piece, logsum + total), (state, logsum))

    zero_state = jnp.zeros((heads, width, width), jnp.float32)
    zero_log = jnp.zeros((heads,), jnp.float32)
    (dev_state, dev_log), (prefix, prefix_log) = lax.scan(
        key_step, (zero_state, zero_log), (totals, contrib)
    )
    return (key_blk, value_blk, cumul, totals, after, prefix, prefix_log, dev_state, dev_log)


def query_side(query_loc, grad_loc, cumul, totals):
    blocks, length, heads = cumul.shape
    width = query_loc.shape[1] // heads
    query_blk = query_loc.reshape(blocks, length, heads, width)
    grad_blk = grad_loc.reshape(blocks, length, heads, width)
    before = jnp.exp(cumul)
    updates = split_left("ntha,nthb->nhab", before[..., None] * widen(query_blk), grad_blk)

    def query_step(carry, item):
        adjoint, logsum = carry
        total, piece = item
        return (
            (jnp.exp(total)[:, None, None] * adjoint + piece, logsum + total),
            (adjoint, logsum),
        )

    zero_state = jnp.zeros((heads, width, width), jnp.float32)
    zero_log = jnp.zeros((heads,), jnp.float32)
    (dev_adjoint, unused), (suffix, suffix_log) = lax.scan(
        query_step, (zero_state, zero_log), (totals, updates), reverse=True
    )
    return (query_blk, grad_blk, before, suffix, suffix_log, dev_adjoint)


def finish(
    query_blk,
    key_blk,
    value_blk,
    grad_blk,
    cumul,
    after,
    before,
    prefix,
    prefix_log,
    suffix,
    suffix_log,
    start_state,
    start_adjoint,
):
    state_prev = jnp.exp(prefix_log)[:, :, None, None] * start_state[None] + prefix
    adjoint = jnp.exp(suffix_log)[:, :, None, None] * start_adjoint[None] + suffix
    blocks, length, heads = cumul.shape
    width = key_blk.shape[3]
    heads_first = jnp.transpose(cumul, (0, 2, 1))
    spread = heads_first[:, :, :, None] - heads_first[:, :, None, :]
    causal = lax.broadcasted_iota(jnp.int32, (length, length), 1) <= lax.broadcasted_iota(
        jnp.int32, (length, length), 0
    )
    weights = jnp.where(
        causal[None, None], jnp.exp(jnp.where(causal[None, None], spread, 0.0)), 0.0
    )
    grad_scores = product("nthd,nshd->nhts", grad_blk, value_blk)
    key_scores = product("nthd,nshd->nhts", query_blk, key_blk)
    first = (weights * grad_scores).astype(jnp.bfloat16)
    second = (weights * key_scores).astype(jnp.bfloat16)
    query_part = product("nhts,nshd->nthd", first, key_blk)
    key_part = product("nhts,nthd->nshd", first, query_blk)
    value_part = product("nhts,nthd->nshd", second, grad_blk)
    grad_query = query_part + before[..., None] * split_right(
        "nthb,nhab->ntha", grad_blk, state_prev
    )
    adj_high, adj_low = halves(adjoint)
    grad_key = key_part + after[..., None] * (
        product("nshb,nhab->nsha", value_blk, adj_high)
        + product("nshb,nhab->nsha", value_blk, adj_low)
    )
    grad_value = value_part + after[..., None] * (
        product("nsha,nhab->nshb", key_blk, adj_high) + product("nsha,nhab->nshb", key_blk, adj_low)
    )
    rows = blocks * length
    flat_query = grad_query.astype(jnp.bfloat16).reshape(rows, heads * width)
    flat_key = grad_key.astype(jnp.bfloat16).reshape(rows, heads * width)
    flat_value = grad_value.astype(jnp.bfloat16).reshape(rows, heads * width)
    return (flat_query, flat_key, flat_value)


def body(queries, keys, values, out_grad, log_decay):
    query_loc, key_loc, value_loc, grad_loc, decay_loc = (
        lax.all_to_all(queries, "exp", split_axis=1, concat_axis=0, tiled=True),
        lax.all_to_all(keys, "exp", split_axis=1, concat_axis=0, tiled=True),
        lax.all_to_all(values, "exp", split_axis=1, concat_axis=0, tiled=True),
        lax.all_to_all(out_grad, "exp", split_axis=1, concat_axis=0, tiled=True),
        lax.all_to_all(log_decay, "exp", split_axis=1, concat_axis=0, tiled=True),
    )
    key_blk, value_blk, cumul, totals, after, prefix, prefix_log, dev_state, dev_log = key_side(
        key_loc, value_loc, decay_loc
    )
    heads = cumul.shape[2]
    width = key_blk.shape[3]
    zero_state = jnp.zeros((heads, width, width), jnp.float32)
    zero_log = jnp.zeros((heads,), jnp.float32)
    start_state = carried_in((dev_log, dev_state), SEQ, link, (zero_log, zero_state), False)[1]
    query_blk, grad_blk, before, suffix, suffix_log, dev_adjoint = query_side(
        query_loc, grad_loc, cumul, totals
    )
    start_adjoint = carried_in((dev_log, dev_adjoint), SEQ, link, (zero_log, zero_state), True)[1]
    flat_query, flat_key, flat_value = finish(
        query_blk,
        key_blk,
        value_blk,
        grad_blk,
        cumul,
        after,
        before,
        prefix,
        prefix_log,
        suffix,
        suffix_log,
        start_state,
        start_adjoint,
    )
    result = (
        lax.all_to_all(flat_query, "exp", split_axis=0, concat_axis=1, tiled=True),
        lax.all_to_all(flat_key, "exp", split_axis=0, concat_axis=1, tiled=True),
        lax.all_to_all(flat_value, "exp", split_axis=0, concat_axis=1, tiled=True),
    )
    return result


def solution(mesh):
    torus = Mesh(mesh.devices.reshape(4, 8, mesh.shape["exp"]), ("seq_0", "seq_1", "exp"))
    placed = (
        P(SEQ_EXP, None),
        P(SEQ_EXP, None),
        P(SEQ_EXP, None),
        P(SEQ_EXP, None),
        P(SEQ_EXP, None),
    )
    return jax.shard_map(
        body,
        mesh=torus,
        in_specs=placed,
        out_specs=(P(SEQ_EXP, None), P(SEQ_EXP, None), P(SEQ_EXP, None)),
        check_vma=False,
    )
```

profile of v0, /device:TPU:1, one launch (start us, length us, event | category | flops | bytes accessed | tf_op | source)
XLA Modules:
  0.0 307.2 jit_solution(12512901773788062015)
XLA Ops:
  7.2 6.5 %all-to-all-start = ((bf16[128,8,4]{0,2,1:T(4,128)(2,1)}), bf16[128,8,4]{0,2,1:T(4,128)(2,1)S(1)}, u32[]{:S(2)}, u32[]{:S(2)}) async-start(bf16[128,8,4]{0,2,1:T(4,128)(2,1)} %bitcast.362), calls=%async_computation | async-start | bytes 16384 | tf_op jit(solution)/shard_map/all_to_all | solution.py:168
  13.7 2.3 copy.61
  16.0 2.3 all-to-all-done
  18.3 4.2 %all-to-all-start.2 = ((bf16[128,8,512]{0,2,1:T(8,128)(2,1)}), bf16[128,8,512]{0,2,1:T(8,128)(2,1)S(1)}, u32[]{:S(2)}, u32[]{:S(2)}) async-start(bf16[128,8,512]{0,2,1:T(8,128)(2,1)} %bitcast.6), calls=%async_computation.2 | async-start | bytes 2097152 | tf_op jit(solution)/shard_map/all_to_all | solution.py:166
  22.5 1.3 copy.105
  23.8 13.8 %all-to-all-done.2 = bf16[128,8,512]{0,2,1:T(8,128)(2,1)S(1)} async-done(((bf16[128,8,512]{0,2,1:T(8,128)(2,1)}), bf16[128,8,512]{0,2,1:T(8,128)(2,1)S(1)}, u32[]{:S(2)}, u32[]{:S(2)}) %all-to-all-start.2) | async-done | bytes 1048608 | tf_op jit(solution)/shard_map/all_to_all | solution.py:166
  38.5 4.3 %all-to-all-start.3 = ((bf16[128,8,512]{0,2,1:T(8,128)(2,1)}), bf16[128,8,512]{0,2,1:T(8,128)(2,1)S(1)}, u32[]{:S(2)}, u32[]{:S(2)}) async-start(bf16[128,8,512]{0,2,1:T(8,128)(2,1)} %bitcast.9), calls=%async_computation.3 | async-start | bytes 2097152 | tf_op jit(solution)/shard_map/all_to_all | solution.py:165
  42.9 1.3 copy.60
  44.2 2.3 copy.107
  46.7 23.3 %fusion.89 = f32[8,128,4]{2,0,1:T(8,128)S(1)} fusion(f32[8,128,4]{2,0,1:T(8,128)S(1)} %copy.57), kind=kOutput, calls=%fused_computation.176 | output fusion | flops 520192 | bytes 32768 | tf_op jit(solution)/shard_map/jit(cumsum)/reduce_window_sum | solution.py:68
  70.2 4.8 %all-to-all-start.1 = ((bf16[128,8,512]{0,2,1:T(8,128)(2,1)}), bf16[128,8,512]{0,2,1:T(8,128)(2,1)S(1)}, u32[]{:S(2)}, u32[]{:S(2)}) async-start(bf16[128,8,512]{0,2,1:T(8,128)(2,1)} %bitcast.358), calls=%async_computation.1 | async-start | bytes 2097152 | tf_op jit(solution)/shard_map/all_to_all | solution.py:167
  75.0 1.1 fusion.88
  76.2 1.2 copy.68
  77.4 1.2 copy.65
  78.6 2.2 fusion.18
  80.8 2.2 convolution_add_fusion.1
  83.0 7.1 %all-to-all-done.1 = bf16[128,8,512]{0,2,1:T(8,128)(2,1)S(1)} async-done(((bf16[128,8,512]{0,2,1:T(8,128)(2,1)}), bf16[128,8,512]{0,2,1:T(8,128)(2,1)S(1)}, u32[]{:S(2)}, u32[]{:S(2)}) %all-to-all-start.1) | async-done | bytes 1048608 | tf_op jit(solution)/shard_map/all_to_all | solution.py:167
  90.1 5.0 %all-to-all-start.5 = ((bf16[128,8,512]{0,2,1:T(8,128)(2,1)}), bf16[128,8,512]{0,2,1:T(8,128)(2,1)}, u32[]{:S(2)}, u32[]{:S(2)}) async-start(bf16[128,8,512]{0,2,1:T(8,128)(2,1)} %bitcast.357), calls=%async_computation.5 | async-start | bytes 2097152 | tf_op jit(solution)/shard_map/all_to_all | solution.py:164
  95.1 1.6 broadcast_in_dim.43.clone
  96.8 14.8 %while.38 = (s32[]{:T(128)}, f32[4,128,128]{2,1,0:T(8,128)S(1)}, f32[4]{0:T(128)S(1)}, f32[8,4,128,128]{3,2,1,0:T(8,128)}, f32[8,4]{1,0:T(8,128)S(1)}, /*index=5...) while((s32[]{:T(128)}, f32[4,128,128]{2,1,0:T(8,128)S(1)}, ...), condition=%wide.region_2.3_spmd.clone, body=%wide.region_1.2_spmd.clone.sunk | while | flops 262155 | bytes 1310977 | solution.py:80
  97.5 1.0 bitcast_add_fusion.13
  99.4 1.0 bitcast_add_fusion.13
  101.2 1.0 bitcast_add_fusion.13
  103.0 1.0 bitcast_add_fusion.13
  104.9 1.0 bitcast_add_fusion.13
  112.4 2.1 fusion.20
  114.4 3.4 %convolution_add_fusion = f32[8,4,128,128]{3,2,1,0:T(8,128)} fusion(f32[8,4,128,128]{3,2,1,0:T(8,128)S(1)} %fusion.20, bf16[8,128,4,128]{1,3,2,0:T(8,128)(2,1)S(1)} %bitcast.345, bf16[8,128,4,128]{1,3,2,0:T(8,128)(2,1)} %bitcast.46, f32[8,128,4]{1,2,0:T(4,128)S(1)} %copy.65), kind=kOutput, calls=%fused_computation.40 | convolution fusion | flops 137887744 | bytes 6307840 | tf_op jit(solution)/shard_map/ntha,nthb->nhab/dot_general | solution.py:44
  118.1 9.3 %while.39 = (s32[]{:T(128)}, f32[4,128,128]{2,1,0:T(8,128)S(1)}, f32[4]{0:T(128)S(1)}, f32[8,4,128,128]{3,2,1,0:T(8,128)S(1)}, f32[8,4]{1,0:T(8,128)S(1)}, /*ind...) while((s32[]{:T(128)}, f32[4,128,128]{2,1,0:T(8,128)S(1)}, ...), condition=%wide.region_4.5_spmd.clone, body=%wide.region_3.4_spmd.clone.sunk | while | flops 262156 | bytes 1310997 | solution.py:104
  118.2 1.0 bitcast_add_fusion.14
  119.3 1.0 bitcast_add_fusion.14
  120.5 1.0 bitcast_add_fusion.14
  121.6 1.0 bitcast_add_fusion.14
  122.8 1.0 bitcast_add_fusion.14
  124.0 1.0 bitcast_add_fusion.14
  125.1 1.0 bitcast_add_fusion.14
  126.3 1.0 bitcast_add_fusion.14
  129.6 16.9 %all-reduce = f32[32]{0:T(128)S(1)} all-reduce(f32[32]{0:T(128)S(1)} %dynamic-update-slice), channel_id=2, replica_groups=mesh['seq_0'=4,'seq_1'=8,'exp'=8] {'seq_1'}, use_global_device_ids=true, to_apply=%add | all-reduce | flops 32 | bytes 256
  146.8 5.6 %all-gather.14.cloned.1.call-done = f32[32,128,128]{2,1,0:T(8,128)} async-done(((f32[4,128,128]{2,1,0:T(8,128)}), f32[32,128,128]{2,1,0:T(8,128)}) %all-gather.14.cloned.1.call-update) | async-done | bytes 2097168 | tf_op jit(solution)/shard_map/all_gather | solution.py:23
  152.4 2.5 fusion.56
  155.0 1.2 copy.58
  156.3 7.4 %all-gather.3 = f32[4,1,4]{2,1,0:T(1,128)S(1)} all-gather(f32[1,1,4]{2,1,0:T(1,128)S(1)} %get-tuple-element.336), channel_id=1, replica_groups=mesh['seq_0'=4,'seq_1'=8,'exp'=8] {'seq_0'}, dimensions={0}, use_global_device_ids=true | all-gather | bytes 80 | tf_op jit(solution)/shard_map/all_gather | solution.py:23
  163.7 5.2 %all-gather.4 = f32[4,1,4]{2,1,0:T(1,128)S(1)} all-gather(f32[1,1,4]{2,1,0:T(1,128)S(1)} %get-tuple-element.335), channel_id=1, replica_groups=mesh['seq_0'=4,'seq_1'=8,'exp'=8] {'seq_0'}, dimensions={0}, use_global_device_ids=true | all-gather | bytes 80 | tf_op jit(solution)/shard_map/all_gather | solution.py:23
  168.9 3.5 %multiply_convert_fusion.1 = bf16[8,4,128,128]{3,2,1,0:T(8,128)(2,1)} fusion(bf16[8,128,4,128]{1,3,2,0:T(8,128)(2,1)} %bitcast.346, bf16[8,128,4,128]{1,3,2,0:T(8,128)(2,1)} %bitcast.351, f32[8,4,128]{2,1,0:T(4,128)S(1)} %copy.58, pred[128,128]{1,0:T(8,128)(4,1)S(1)} %iota_compare_fusion), kind=kOutput, calls=%fused_computation.36 | convolution fusion | flops 136839168 | bytes 3178496 | tf_op jit(solution)/shard_map/nthd,nshd->nhts/dot_general | solution.py:44
  172.4 21.3 %all-gather.16.cloned.1.call-done = f32[32,128,128]{2,1,0:T(8,128)} async-done(((f32[4,128,128]{2,1,0:T(8,128)}), f32[32,128,128]{2,1,0:T(8,128)}) %all-gather.16.cloned.1.call-update) | async-done | bytes 2097168 | tf_op jit(solution)/shard_map/all_gather | solution.py:23
  193.7 2.4 fusion.44
  196.2 3.5 %fusion.90 = f32[8,4,128,128]{2,3,1,0:T(8,128)} fusion(bf16[8,4,128,128]{3,2,1,0:T(8,128)(2,1)} %multiply_convert_fusion.1, bf16[8,128,4,128]{1,3,2,0:T(8,128)(2,1)S(1)} %bitcast.340), kind=kOutput, calls=%fused_computation.177 | convolution fusion | flops 134217728 | bytes 4194304 | tf_op jit(solution)/shard_map/nhts,nshd->nthd/dot_general | solution.py:44
  199.7 23.7 %all-gather.10.cloned.1.call-done = f32[4,4,128,128]{3,2,1,0:T(8,128)} async-done(((f32[1,4,128,128]{3,2,1,0:T(8,128)}), f32[4,4,128,128]{3,2,1,0:T(8,128)}) %all-gather.10.cloned.1.call-update) | async-done | bytes 1048592 | tf_op jit(solution)/shard_map/all_gather | solution.py:23
  223.4 2.4 fusion.55
  226.7 1.1 copy-done.8
  227.8 1.7 fusion.13
  229.5 5.9 %all-to-all-start.4 = ((bf16[8,128,512]{1,2,0:T(8,128)(2,1)}), bf16[8,128,512]{1,2,0:T(8,128)(2,1)}, u32[]{:S(2)}, u32[]{:S(2)}) async-start(bf16[8,128,512]{1,2,0:T(8,128)(2,1)} %bitcast.360), calls=%async_computation.4 | async-start | bytes 2097152 | tf_op jit(solution)/shard_map/all_to_all | solution.py:198
  235.3 16.6 %all-gather.12.cloned.1.call-done = f32[4,4,128,128]{3,2,1,0:T(8,128)} async-done(((f32[1,4,128,128]{3,2,1,0:T(8,128)}), f32[4,4,128,128]{3,2,1,0:T(8,128)}) %all-gather.12.cloned.1.call-update) | async-done | bytes 1048592 | tf_op jit(solution)/shard_map/all_gather | solution.py:23
  251.9 2.3 fusion.43
  256.0 2.8 fusion.11
  258.8 5.9 %all-to-all-start.6 = ((bf16[8,128,512]{1,2,0:T(8,128)(2,1)}), bf16[8,128,512]{1,2,0:T(8,128)(2,1)}, u32[]{:S(2)}, u32[]{:S(2)}) async-start(bf16[8,128,512]{1,2,0:T(8,128)(2,1)} %bitcast.356), calls=%async_computation.6 | async-start | bytes 2097152 | tf_op jit(solution)/shard_map/all_to_all | solution.py:199
  264.7 2.1 fusion.36
  266.8 2.1 fusion.84
  268.9 5.1 %fusion.9 = bf16[8,128,4,128]{1,3,2,0:T(8,128)(2,1)} fusion(f32[8,4,128,128]{3,2,1,0:T(8,128)} %fusion.36, f32[8,4,128,128]{3,2,1,0:T(8,128)} %fusion.84, bf16[8,128,4,128]{1,3,2,0:T(8,128)(2,1)} %bitcast.347, bf16[8,128,4,128]{1,3,2,0:T(8,128)(2,1)} %bitcast.46, bf16[8,128,4,128]{1,3,2,0:T(8,128)(2,1)S(1)} %bitcast.343, f32[8,128,4]{1,2,0:T(4,128)S(1)} %copy.68, ...), kind=kOutput, calls=%fused_computation.18 | convolution fusion | flops 273154048 | bytes 8437760 | tf_op jit(solution)/shard_map/nhts,nthd->nshd/dot_general | solution.py:44
  274.0 5.9 %all-to-all-done.6 = bf16[8,128,512]{1,2,0:T(8,128)(2,1)} async-done(((bf16[8,128,512]{1,2,0:T(8,128)(2,1)}), bf16[8,128,512]{1,2,0:T(8,128)(2,1)}, u32[]{:S(2)}, u32[]{:S(2)}) %all-to-all-start.6) | async-done | bytes 1048608 | tf_op jit(solution)/shard_map/all_to_all | solution.py:199
  279.9 4.3 %all-to-all-start.7 = ((bf16[8,128,512]{1,2,0:T(8,128)(2,1)}), bf16[8,128,512]{1,2,0:T(8,128)(2,1)S(1)}, u32[]{:S(2)}, u32[]{:S(2)}) async-start(bf16[8,128,512]{1,2,0:T(8,128)(2,1)} %bitcast.69), calls=%async_computation.7 | async-start | bytes 2097152 | tf_op jit(solution)/shard_map/all_to_all | solution.py:200
  284.2 2.3 copy.106
  286.5 2.3 copy.108
  288.7 10.6 %all-to-all-done.7 = bf16[8,128,512]{1,2,0:T(8,128)(2,1)S(1)} async-done(((bf16[8,128,512]{1,2,0:T(8,128)(2,1)}), bf16[8,128,512]{1,2,0:T(8,128)(2,1)S(1)}, u32[]{:S(2)}, u32[]{:S(2)}) %all-to-all-start.7) | async-done | bytes 1048608 | tf_op jit(solution)/shard_map/all_to_all | solution.py:200
  299.3 1.3 copy.109
  (118 shorter events, 17.1 us)
Async XLA Ops:
  7.2 11.1 %all-to-all-start = ((bf16[128,8,4]{0,2,1:T(4,128)(2,1)}), bf16[128,8,4]{0,2,1:T(4,128)(2,1)S(1)}, u32[]{:S(2)}, u32[]{:S(2)}) async-start(bf16[128,8,4]{0,2,1:T(4,128)(2,1)} %bitcast.362), calls=%async_computation | async-start | bytes 16384 | tf_op jit(solution)/shard_map/all_to_all | solution.py:168
  13.6 8.8 %copy-start.12 = (bf16[128,4096]{1,0:T(8,128)(2,1)S(1)}, bf16[128,4096]{1,0:T(8,128)(2,1)}, u32[]{:S(2)}) copy-start(bf16[128,4096]{1,0:T(8,128)(2,1)} %param.10) | copy-start | bytes 3145732
  18.3 19.3 %all-to-all-start.2 = ((bf16[128,8,512]{0,2,1:T(8,128)(2,1)}), bf16[128,8,512]{0,2,1:T(8,128)(2,1)S(1)}, u32[]{:S(2)}, u32[]{:S(2)}) async-start(bf16[128,8,512]{0,2,1:T(8,128)(2,1)} %bitcast.6), calls=%async_computation.2 | async-start | bytes 2097152 | tf_op jit(solution)/shard_map/all_to_all | solution.py:166
  22.4 20.4 %copy-start.13 = (bf16[128,4096]{1,0:T(8,128)(2,1)S(1)}, bf16[128,4096]{1,0:T(8,128)(2,1)}, u32[]{:S(2)}) copy-start(bf16[128,4096]{1,0:T(8,128)(2,1)} %param.12) | copy-start | bytes 3145732
  37.6 1.0 copy-start.4
  38.5 31.7 %all-to-all-start.3 = ((bf16[128,8,512]{0,2,1:T(8,128)(2,1)}), bf16[128,8,512]{0,2,1:T(8,128)(2,1)S(1)}, u32[]{:S(2)}, u32[]{:S(2)}) async-start(bf16[128,8,512]{0,2,1:T(8,128)(2,1)} %bitcast.9), calls=%async_computation.3 | async-start | bytes 2097152 | tf_op jit(solution)/shard_map/all_to_all | solution.py:165
  70.0 7.4 %copy-start.9 = (f32[8,128,4]{2,0,1:T(8,128)}, f32[8,128,4]{2,0,1:T(8,128)S(1)}, u32[]{:S(2)}) copy-start(f32[8,128,4]{2,0,1:T(8,128)S(1)} %fusion.89) | copy-start | bytes 49156
  70.2 19.9 %all-to-all-start.1 = ((bf16[128,8,512]{0,2,1:T(8,128)(2,1)}), bf16[128,8,512]{0,2,1:T(8,128)(2,1)S(1)}, u32[]{:S(2)}, u32[]{:S(2)}) async-start(bf16[128,8,512]{0,2,1:T(8,128)(2,1)} %bitcast.358), calls=%async_computation.1 | async-start | bytes 2097152 | tf_op jit(solution)/shard_map/all_to_all | solution.py:167
  78.6 2.2 copy-start.5
  90.1 24.3 %copy-start = (bf16[128,8,512]{0,2,1:T(8,128)(2,1)}, bf16[128,8,512]{0,2,1:T(8,128)(2,1)S(1)}, u32[]{:S(2)}) copy-start(bf16[128,8,512]{0,2,1:T(8,128)(2,1)S(1)} %all-to-all-done.1) | copy-start | bytes 3145732
  90.1 22.2 %all-to-all-start.5 = ((bf16[128,8,512]{0,2,1:T(8,128)(2,1)}), bf16[128,8,512]{0,2,1:T(8,128)(2,1)}, u32[]{:S(2)}, u32[]{:S(2)}) async-start(bf16[128,8,512]{0,2,1:T(8,128)(2,1)} %bitcast.357), calls=%async_computation.5 | async-start | bytes 2097152 | tf_op jit(solution)/shard_map/all_to_all | solution.py:164
  95.1 57.2 %all-gather.14.cloned.1.call-start = ((), (), s32[]{:S(2)}) async-start(), calls=%async_computation.10 | async-start | bytes 2359296 | tf_op jit(solution)/shard_map/all_gather | solution.py:23
  111.6 0.7 copy-start.3
  112.3 81.4 %all-gather.16.cloned.1.call-start = ((), (), s32[]{:S(2)}) async-start(), calls=%async_computation.11 | async-start | bytes 2359296 | tf_op jit(solution)/shard_map/all_gather | solution.py:23
  118.1 10.1 %copy-start.14 = (u32[256]{0:T(256)S(1)}, u32[256]{0:T(256)}, u32[]{:S(2)}) copy-start(u32[256]{0:T(256)} %constant.92) | copy-start | bytes 3076
  127.4 0.7 copy-start.2
  128.1 95.3 %all-gather.10.cloned.1.call-start = ((), (), s32[]{:S(2)}) async-start(), calls=%async_computation.8 | async-start | bytes 1310720 | tf_op jit(solution)/shard_map/all_gather | solution.py:23
  154.9 97.0 %all-gather.12.cloned.1.call-start = ((), (), s32[]{:S(2)}) async-start(), calls=%async_computation.9 | async-start | bytes 1310720 | tf_op jit(solution)/shard_map/all_gather | solution.py:23
  196.2 27.2 %copy-start.11 = (f32[1,4,128,128]{3,2,1,0:T(8,128)S(1)}, f32[1,4,128,128]{3,2,1,0:T(8,128)}, u32[]{:S(2)}) copy-start(f32[1,4,128,128]{3,2,1,0:T(8,128)} %get-tuple-element.313) | copy-start | bytes 786436
  223.4 2.4 copy-start.1
  223.4 2.8 copy-start.7
  226.2 1.6 copy-start.8
  229.5 29.3 %all-to-all-start.4 = ((bf16[8,128,512]{1,2,0:T(8,128)(2,1)}), bf16[8,128,512]{1,2,0:T(8,128)(2,1)}, u32[]{:S(2)}, u32[]{:S(2)}) async-start(bf16[8,128,512]{1,2,0:T(8,128)(2,1)} %bitcast.360), calls=%async_computation.4 | async-start | bytes 2097152 | tf_op jit(solution)/shard_map/all_to_all | solution.py:198
  251.9 2.3 copy-start.6
  254.8 1.2 copy-start.10
  258.8 21.1 %all-to-all-start.6 = ((bf16[8,128,512]{1,2,0:T(8,128)(2,1)}), bf16[8,128,512]{1,2,0:T(8,128)(2,1)}, u32[]{:S(2)}, u32[]{:S(2)}) async-start(bf16[8,128,512]{1,2,0:T(8,128)(2,1)} %bitcast.356), calls=%async_computation.6 | async-start | bytes 2097152 | tf_op jit(solution)/shard_map/all_to_all | solution.py:199
  279.9 19.4 %all-to-all-start.7 = ((bf16[8,128,512]{1,2,0:T(8,128)(2,1)}), bf16[8,128,512]{1,2,0:T(8,128)(2,1)S(1)}, u32[]{:S(2)}, u32[]{:S(2)}) async-start(bf16[8,128,512]{1,2,0:T(8,128)(2,1)} %bitcast.69), calls=%async_computation.7 | async-start | bytes 2097152 | tf_op jit(solution)/shard_map/all_to_all | solution.py:200
Sparse Core Ops, SparseCore 0:
  112.4 39.9 all-gather.13
  154.2 39.4 all-gather.15
  195.5 27.8 all-gather.9
  225.1 26.8 all-gather.11
where the time goes:
time: 309 us; the launch traced here: 307 us
  waiting for transfers between devices  107 us (35%)
  other arithmetic  57.4 us (19%)
  starting transfers between devices  41 us (13%)
  matrix products  32.2 us (10%)
  blocking collectives  29.5 us (10%)
  local copies, waits for them, and re-layouts  25.1 us (8%)
  between operations  14.7 us (5%)
    all_gather x4, waiting for transfers between devices, carried_in(): pieces = jax.tree.map(lambda part: lax.all_gather(part, axis), total)  67.3 us
    dot_general x14, matrix products, product(): jnp.einsum(form, first_op, second_op, preferred_element_type=jnp.float32)  32.2 us
    another operation x1, other arithmetic, key_side(): cumul = jnp.cumsum(widen(decay_loc).reshape(blocks, BLOCK, heads), axis=1)  23.3 us
    unnamed x1, blocking collectives  16.9 us
    all_to_all x1, waiting for transfers between devices, body(): lax.all_to_all(values, 'exp', split_axis=1, concat_axis=0, tiled=True)  13.8 us
    all_gather x2, blocking collectives, carried_in(): pieces = jax.tree.map(lambda part: lax.all_gather(part, axis), total)  12.5 us
    all_to_all x1, waiting for transfers between devices, body(): lax.all_to_all(flat_value, 'exp', split_axis=0, concat_axis=1, tiled=True)  10.6 us
    unnamed x36, local copies, waits for them, and re-layouts  9.1 us
  transfers between devices with their start and end apart: 12, of which 9 were waited for; matrix products, arithmetic and copies ran while one was open for 35% of the time, Pallas kernels for 0%

commit v1 on v0

--- a/solution.py
+++ b/solution.py
@@ -164,7 +164,12 @@
         lax.all_to_all(queries, "exp", split_axis=1, concat_axis=0, tiled=True),
         lax.all_to_all(keys, "exp", split_axis=1, concat_axis=0, tiled=True),
         lax.all_to_all(values, "exp", split_axis=1, concat_axis=0, tiled=True),
-        lax.all_to_all(out_grad, "exp", split_axis=1, concat_axis=0, tiled=True),
+        jnp.concatenate(
+            lax.all_to_all(
+                jnp.stack(jnp.split(out_grad, lax.axis_size("exp"), axis=1)), "exp", 0, 0
+            ),
+            axis=0,
+        ),
         lax.all_to_all(log_decay, "exp", split_axis=1, concat_axis=0, tiled=True),
     )
     key_blk, value_blk, cumul, totals, after, prefix, prefix_log, dev_state, dev_log = key_side(

time: 309 us -> 298 us (0.964)
  other arithmetic: 57.4 us -> 35.3 us
  waiting for transfers between devices: 107 us -> 118 us
    another operation x1, other arithmetic: 23.3 us -> 1.18 us  [key_side(): cumul = jnp.cumsum(widen(decay_loc).reshape(blocks, BLOCK, heads), axis=1)]
    all_to_all x1, waiting for transfers between devices: 0.01 us -> 11.4 us  [body(): lax.all_to_all(keys, 'exp', split_axis=1, concat_axis=0, tiled=True)]
    unnamed x36 -> x50, local copies, waits for them, and re-layouts: 9.1 us -> 7.26 us
  transfers between devices with their start and end apart: 12 -> 12, of which waited for: 9 -> 9; matrix products, arithmetic and copies ran while one was open for 35% -> 29% of each run, Pallas kernels for 0% -> 0%
where the time goes in v1:
time: 298 us; the launch traced here: 297 us
  waiting for transfers between devices  118 us (40%)
  starting transfers between devices  41.2 us (14%)
  other arithmetic  35.3 us (12%)
  blocking collectives  30.8 us (10%)
  matrix products  29.9 us (10%)
  local copies, waits for them, and re-layouts  26.2 us (9%)
  between operations  14.9 us (5%)
    all_gather x4, waiting for transfers between devices, carried_in(): pieces = jax.tree.map(lambda part: lax.all_gather(part, axis), total)  64.6 us
    dot_general x14, matrix products, product(): jnp.einsum(form, first_op, second_op, preferred_element_type=jnp.float32)  29.9 us
    unnamed x1, blocking collectives  17.3 us
    all_to_all x1, waiting for transfers between devices, body(): lax.all_to_all(values, 'exp', split_axis=1, concat_axis=0, tiled=True)  15 us
    all_gather x2, blocking collectives, carried_in(): pieces = jax.tree.map(lambda part: lax.all_gather(part, axis), total)  13.5 us
    all_to_all x1, waiting for transfers between devices, body(): lax.all_to_all(keys, 'exp', split_axis=1, concat_axis=0, tiled=True)  11.4 us
    all_to_all x1, waiting for transfers between devices, body(): lax.all_to_all(flat_value, 'exp', split_axis=0, concat_axis=1, tiled=True)  10.6 us
    all_to_all x1, waiting for transfers between devices, body(): lax.all_to_all(jnp.stack(jnp.split(out_grad, lax.axis_size('exp'), axis=1...  8.57 us
  transfers between devices with their start and end apart: 12, of which 9 were waited for; matrix products, arithmetic and copies ran while one was open for 29% of the time, Pallas kernels for 0%

profile of v1, /device:TPU:1, one launch (start us, length us, event | category | flops | bytes accessed | tf_op | source)
XLA Modules:
  0.0 296.6 jit_solution(7164270519263058525)
XLA Ops:
  7.2 6.5 %all-to-all-start = ((bf16[128,8,4]{0,2,1:T(4,128)(2,1)}), bf16[128,8,4]{0,2,1:T(4,128)(2,1)S(1)}, u32[]{:S(2)}, u32[]{:S(2)}) async-start(bf16[128,8,4]{0,2,1:T(4,128)(2,1)} %bitcast.374), calls=%async_computation | async-start | bytes 16384 | tf_op jit(solution)/shard_map/all_to_all | solution.py:173
  13.7 1.4 fusion.88
  16.2 1.3 copy.75
  17.5 2.3 copy.119
  19.9 1.3 copy.121
  21.2 4.8 %all-to-all-start.2 = ((bf16[128,8,512]{0,2,1:T(8,128)(2,1)}), bf16[128,8,512]{0,2,1:T(8,128)(2,1)S(1)}, u32[]{:S(2)}, u32[]{:S(2)}) async-start(bf16[128,8,512]{0,2,1:T(8,128)(2,1)} %bitcast.12), calls=%async_computation.2 | async-start | bytes 2097152 | tf_op jit(solution)/shard_map/all_to_all | solution.py:166
  26.1 15.0 %all-to-all-done.2 = bf16[128,8,512]{0,2,1:T(8,128)(2,1)S(1)} async-done(((bf16[128,8,512]{0,2,1:T(8,128)(2,1)}), bf16[128,8,512]{0,2,1:T(8,128)(2,1)S(1)}, u32[]{:S(2)}, u32[]{:S(2)}) %all-to-all-start.2) | async-done | bytes 1048608 | tf_op jit(solution)/shard_map/all_to_all | solution.py:166
  41.1 4.3 %all-to-all-start.3 = ((bf16[128,8,512]{0,2,1:T(8,128)(2,1)}), bf16[128,8,512]{0,2,1:T(8,128)(2,1)S(1)}, u32[]{:S(2)}, u32[]{:S(2)}) async-start(bf16[128,8,512]{0,2,1:T(8,128)(2,1)} %bitcast.369), calls=%async_computation.3 | async-start | bytes 2097152 | tf_op jit(solution)/shard_map/all_to_all | solution.py:165
  47.8 1.2 fusion.90
  49.2 11.4 %all-to-all-done.3 = bf16[128,8,512]{0,2,1:T(8,128)(2,1)S(1)} async-done(((bf16[128,8,512]{0,2,1:T(8,128)(2,1)}), bf16[128,8,512]{0,2,1:T(8,128)(2,1)S(1)}, u32[]{:S(2)}, u32[]{:S(2)}) %all-to-all-start.3) | async-done | bytes 1048608 | tf_op jit(solution)/shard_map/all_to_all | solution.py:165
  60.5 5.0 %all-to-all-start.1 = ((bf16[8,128,512]{1,2,0:T(8,128)(2,1)}), bf16[8,128,512]{1,2,0:T(8,128)(2,1)}, u32[]{:S(2)}, u32[]{:S(2)}) async-start(bf16[8,128,512]{1,2,0:T(8,128)(2,1)} %bitcast_dynamic-update-slice_fusion.2), calls=%async_computation.1 | async-start | bytes 2097152 | tf_op jit(solution)/shard_map/all_to_all | solution.py:168
  65.5 1.1 fusion.89
  66.7 1.2 copy.82
  67.9 1.2 copy.79
  70.0 2.2 convolution_add_fusion.1
  72.2 8.6 %all-to-all-done.1 = bf16[8,128,512]{1,2,0:T(8,128)(2,1)} async-done(((bf16[8,128,512]{1,2,0:T(8,128)(2,1)}), bf16[8,128,512]{1,2,0:T(8,128)(2,1)}, u32[]{:S(2)}, u32[]{:S(2)}) %all-to-all-start.1) | async-done | bytes 1048608 | tf_op jit(solution)/shard_map/all_to_all | solution.py:168
  80.8 4.3 %all-to-all-start.5 = ((bf16[128,8,512]{0,2,1:T(8,128)(2,1)}), bf16[128,8,512]{0,2,1:T(8,128)(2,1)S(1)}, u32[]{:S(2)}, u32[]{:S(2)}) async-start(bf16[128,8,512]{0,2,1:T(8,128)(2,1)} %bitcast.368), calls=%async_computation.5 | async-start | bytes 2097152 | tf_op jit(solution)/shard_map/all_to_all | solution.py:164
  85.1 1.6 broadcast_in_dim.43.clone
  86.7 14.8 %while.38 = (s32[]{:T(128)}, f32[4,128,128]{2,1,0:T(8,128)S(1)}, f32[4]{0:T(128)S(1)}, f32[8,4,128,128]{3,2,1,0:T(8,128)}, f32[8,4]{1,0:T(8,128)S(1)}, /*index=5...) while((s32[]{:T(128)}, f32[4,128,128]{2,1,0:T(8,128)S(1)}, ...), condition=%wide.region_2.3_spmd.clone, body=%wide.region_1.2_spmd.clone.sunk | while | flops 262155 | bytes 1310977 | solution.py:80
  87.5 1.0 bitcast_add_fusion.13
  89.3 1.0 bitcast_add_fusion.13
  91.2 1.0 bitcast_add_fusion.13
  93.0 1.0 bitcast_add_fusion.13
  94.9 1.0 bitcast_add_fusion.13
  96.7 1.0 bitcast_add_fusion.13
  98.6 1.0 bitcast_add_fusion.13
  102.3 2.4 fusion.20
  104.8 3.4 %convolution_add_fusion = f32[8,4,128,128]{3,2,1,0:T(8,128)} fusion(f32[8,4,128,128]{3,2,1,0:T(8,128)S(1)} %fusion.20, bf16[8,128,4,128]{1,3,2,0:T(8,128)(2,1)} %bitcast.11, bf16[8,128,4,128]{1,3,2,0:T(8,128)(2,1)S(1)} %bitcast.363, f32[8,128,4]{1,2,0:T(4,128)S(1)} %copy.79), kind=kOutput, calls=%fused_computation.40 | convolution fusion | flops 137887744 | bytes 6307840 | tf_op jit(solution)/shard_map/ntha,nthb->nhab/dot_general | solution.py:44
  108.5 9.3 %while.39 = (s32[]{:T(128)}, f32[4,128,128]{2,1,0:T(8,128)S(1)}, f32[4]{0:T(128)S(1)}, f32[8,4,128,128]{3,2,1,0:T(8,128)S(1)}, f32[8,4]{1,0:T(8,128)S(1)}, /*ind...) while((s32[]{:T(128)}, f32[4,128,128]{2,1,0:T(8,128)S(1)}, ...), condition=%wide.region_4.5_spmd.clone, body=%wide.region_3.4_spmd.clone.sunk | while | flops 262156 | bytes 1310997 | solution.py:104
  108.5 1.0 bitcast_add_fusion.14
  109.7 1.0 bitcast_add_fusion.14
  110.8 1.0 bitcast_add_fusion.14
  112.0 1.0 bitcast_add_fusion.14
  113.2 1.0 bitcast_add_fusion.14
  114.3 1.0 bitcast_add_fusion.14
  115.5 1.1 bitcast_add_fusion.14
  116.6 1.0 bitcast_add_fusion.14
  120.1 17.3 %all-reduce = f32[32]{0:T(128)S(1)} all-reduce(f32[32]{0:T(128)S(1)} %dynamic-update-slice), channel_id=2, replica_groups=mesh['seq_0'=4,'seq_1'=8,'exp'=8] {'seq_1'}, use_global_device_ids=true, to_apply=%add | all-reduce | flops 32 | bytes 256
  137.6 4.5 %all-gather.14.cloned.1.call-done = f32[32,128,128]{2,1,0:T(8,128)} async-done(((f32[4,128,128]{2,1,0:T(8,128)}), f32[32,128,128]{2,1,0:T(8,128)}) %all-gather.14.cloned.1.call-update) | async-done | bytes 2097168 | tf_op jit(solution)/shard_map/all_gather | solution.py:23
  142.1 2.4 fusion.57
  144.6 1.2 copy.65
  146.0 8.3 %all-gather.3 = f32[4,1,4]{2,1,0:T(1,128)S(1)} all-gather(f32[1,1,4]{2,1,0:T(1,128)S(1)} %get-tuple-element.344), channel_id=1, replica_groups=mesh['seq_0'=4,'seq_1'=8,'exp'=8] {'seq_0'}, dimensions={0}, use_global_device_ids=true | all-gather | bytes 80 | tf_op jit(solution)/shard_map/all_gather | solution.py:23
  154.2 5.2 %all-gather.4 = f32[4,1,4]{2,1,0:T(1,128)S(1)} all-gather(f32[1,1,4]{2,1,0:T(1,128)S(1)} %get-tuple-element.343), channel_id=1, replica_groups=mesh['seq_0'=4,'seq_1'=8,'exp'=8] {'seq_0'}, dimensions={0}, use_global_device_ids=true | all-gather | bytes 80 | tf_op jit(solution)/shard_map/all_gather | solution.py:23
  159.4 3.5 %multiply_convert_fusion.1 = bf16[8,4,128,128]{3,2,1,0:T(8,128)(2,1)} fusion(bf16[8,128,4,128]{1,3,2,0:T(8,128)(2,1)} %bitcast.11, bf16[8,128,4,128]{1,3,2,0:T(8,128)(2,1)} %bitcast.359, f32[8,4,128]{2,1,0:T(4,128)S(1)} %copy.65, pred[128,128]{1,0:T(8,128)(4,1)S(1)} %iota_compare_fusion), kind=kOutput, calls=%fused_computation.36 | convolution fusion | flops 136839168 | bytes 3178496 | tf_op jit(solution)/shard_map/nthd,nshd->nhts/dot_general | solution.py:44
  162.9 20.5 %all-gather.16.cloned.1.call-done = f32[32,128,128]{2,1,0:T(8,128)} async-done(((f32[4,128,128]{2,1,0:T(8,128)}), f32[32,128,128]{2,1,0:T(8,128)}) %all-gather.16.cloned.1.call-update) | async-done | bytes 2097168 | tf_op jit(solution)/shard_map/all_gather | solution.py:23
  183.5 2.5 fusion.45
  186.0 3.4 %fusion.91 = f32[8,4,128,128]{2,3,1,0:T(8,128)} fusion(bf16[8,4,128,128]{3,2,1,0:T(8,128)(2,1)} %multiply_convert_fusion.1, bf16[8,128,4,128]{1,3,2,0:T(8,128)(2,1)S(1)} %bitcast.353), kind=kOutput, calls=%fused_computation.186 | convolution fusion | flops 134217728 | bytes 4194304 | tf_op jit(solution)/shard_map/nhts,nshd->nthd/dot_general | solution.py:44
  189.4 24.3 %all-gather.10.cloned.1.call-done = f32[4,4,128,128]{3,2,1,0:T(8,128)} async-done(((f32[1,4,128,128]{3,2,1,0:T(8,128)}), f32[4,4,128,128]{3,2,1,0:T(8,128)}) %all-gather.10.cloned.1.call-update) | async-done | bytes 1048592 | tf_op jit(solution)/shard_map/all_gather | solution.py:23
  213.7 2.4 fusion.56
  216.2 1.9 fusion.23
  218.1 3.0 %fusion.13 = bf16[8,128,4,128]{1,3,2,0:T(8,128)(2,1)} fusion(f32[8,4,128,128]{2,3,1,0:T(8,128)S(1)} %copy-done.7, f32[8,4,128,128]{3,2,1,0:T(8,128)S(1)} %fusion.23, bf16[8,128,4,128]{1,3,2,0:T(8,128)(2,1)} %bitcast.11, f32[8,4,128,128]{3,2,1,0:T(8,128)S(1)} %copy-done.4, f32[4,128,128]{2,1,0:T(8,128)S(1)} %fusion.56, f32[8,4]{1,0:T(8,128)S(1)} %exp.200, ...), kind=kOutput, calls=%fused_computation.24 | convolution fusion | flops 139460608 | bytes 8667264 | tf_op jit(solution)/shard_map/nthb,nhab->ntha/dot_general | solution.py:44
  221.1 5.9 %all-to-all-start.4 = ((bf16[8,128,512]{1,2,0:T(8,128)(2,1)}), bf16[8,128,512]{1,2,0:T(8,128)(2,1)}, u32[]{:S(2)}, u32[]{:S(2)}) async-start(bf16[8,128,512]{1,2,0:T(8,128)(2,1)} %bitcast.371), calls=%async_computation.4 | async-start | bytes 2097152 | tf_op jit(solution)/shard_map/all_to_all | solution.py:203
  227.0 15.3 %all-gather.12.cloned.1.call-done = f32[4,4,128,128]{3,2,1,0:T(8,128)} async-done(((f32[1,4,128,128]{3,2,1,0:T(8,128)}), f32[4,4,128,128]{3,2,1,0:T(8,128)}) %all-gather.12.cloned.1.call-update) | async-done | bytes 1048592 | tf_op jit(solution)/shard_map/all_gather | solution.py:23
  242.3 2.3 fusion.44
  246.7 1.5 fusion.11
  248.2 5.9 %all-to-all-start.6 = ((bf16[8,128,512]{1,2,0:T(8,128)(2,1)}), bf16[8,128,512]{1,2,0:T(8,128)(2,1)}, u32[]{:S(2)}, u32[]{:S(2)}) async-start(bf16[8,128,512]{1,2,0:T(8,128)(2,1)} %bitcast.367), calls=%async_computation.6 | async-start | bytes 2097152 | tf_op jit(solution)/shard_map/all_to_all | solution.py:204
  254.1 4.0 %fusion.22 = f32[8,4,128,128]{3,2,1,0:T(8,128)} fusion(bf16[8,128,4,128]{1,3,2,0:T(8,128)(2,1)} %bitcast.11, bf16[8,128,4,128]{1,3,2,0:T(8,128)(2,1)} %bitcast.364, bf16[8,128,4,128]{1,3,2,0:T(8,128)(2,1)S(1)} %bitcast.354, f32[8,4,128]{2,1,0:T(4,128)S(1)} %copy.65, pred[128,128]{1,0:T(8,128)(4,1)S(1)} %iota_compare_fusion), kind=kOutput, calls=%fused_computation.44 | convolution fusion | flops 271056896 | bytes 5275648 | tf_op jit(solution)/shard_map/nhts,nthd->nshd/dot_general | solution.py:44
  259.7 1.8 fusion.9
  261.5 7.8 %all-to-all-done.6 = bf16[8,128,512]{1,2,0:T(8,128)(2,1)} async-done(((bf16[8,128,512]{1,2,0:T(8,128)(2,1)}), bf16[8,128,512]{1,2,0:T(8,128)(2,1)}, u32[]{:S(2)}, u32[]{:S(2)}) %all-to-all-start.6) | async-done | bytes 1048608 | tf_op jit(solution)/shard_map/all_to_all | solution.py:204
  269.3 4.3 %all-to-all-start.7 = ((bf16[8,128,512]{1,2,0:T(8,128)(2,1)}), bf16[8,128,512]{1,2,0:T(8,128)(2,1)S(1)}, u32[]{:S(2)}, u32[]{:S(2)}) async-start(bf16[8,128,512]{1,2,0:T(8,128)(2,1)} %bitcast.372), calls=%async_computation.7 | async-start | bytes 2097152 | tf_op jit(solution)/shard_map/all_to_all | solution.py:205
  273.6 2.3 copy.120
  275.9 2.3 copy.122
  278.2 10.6 %all-to-all-done.7 = bf16[8,128,512]{1,2,0:T(8,128)(2,1)S(1)} async-done(((bf16[8,128,512]{1,2,0:T(8,128)(2,1)}), bf16[8,128,512]{1,2,0:T(8,128)(2,1)S(1)}, u32[]{:S(2)}, u32[]{:S(2)}) %all-to-all-start.7) | async-done | bytes 1048608 | tf_op jit(solution)/shard_map/all_to_all | solution.py:205
  288.8 1.3 copy.123
  (134 shorter events, 19.2 us)
Async XLA Ops:
  7.2 14.0 %all-to-all-start = ((bf16[128,8,4]{0,2,1:T(4,128)(2,1)}), bf16[128,8,4]{0,2,1:T(4,128)(2,1)S(1)}, u32[]{:S(2)}, u32[]{:S(2)}) async-start(bf16[128,8,4]{0,2,1:T(4,128)(2,1)} %bitcast.374), calls=%async_computation | async-start | bytes 16384 | tf_op jit(solution)/shard_map/all_to_all | solution.py:173
  13.6 2.5 copy-start.12
  17.5 2.4 copy-start.13
  21.2 19.9 %all-to-all-start.2 = ((bf16[128,8,512]{0,2,1:T(8,128)(2,1)}), bf16[128,8,512]{0,2,1:T(8,128)(2,1)S(1)}, u32[]{:S(2)}, u32[]{:S(2)}) async-start(bf16[128,8,512]{0,2,1:T(8,128)(2,1)} %bitcast.12), calls=%async_computation.2 | async-start | bytes 2097152 | tf_op jit(solution)/shard_map/all_to_all | solution.py:166
  26.1 15.0 %copy-start.11 = (bf16[8,128,512]{1,2,0:T(8,128)(2,1)}, bf16[8,128,512]{1,2,0:T(8,128)(2,1)S(1)}, u32[]{:S(2)}) copy-start(bf16[8,128,512]{1,2,0:T(8,128)(2,1)S(1)} %bitcast_dynamic-update-slice_fusion.4) | copy-start | bytes 3145732
  41.1 28.9 %copy-start.2 = (bf16[128,8,512]{0,2,1:T(8,128)(2,1)}, bf16[128,8,512]{0,2,1:T(8,128)(2,1)S(1)}, u32[]{:S(2)}) copy-start(bf16[128,8,512]{0,2,1:T(8,128)(2,1)S(1)} %all-to-all-done.2) | copy-start | bytes 3145732
  41.1 19.5 %all-to-all-start.3 = ((bf16[128,8,512]{0,2,1:T(8,128)(2,1)}), bf16[128,8,512]{0,2,1:T(8,128)(2,1)S(1)}, u32[]{:S(2)}, u32[]{:S(2)}) async-start(bf16[128,8,512]{0,2,1:T(8,128)(2,1)} %bitcast.369), calls=%async_computation.3 | async-start | bytes 2097152 | tf_op jit(solution)/shard_map/all_to_all | solution.py:165
  49.0 18.9 %copy-start.8 = (f32[8,128,4]{2,0,1:T(8,128)}, f32[8,128,4]{2,0,1:T(8,128)S(1)}, u32[]{:S(2)}) copy-start(f32[8,128,4]{2,0,1:T(8,128)S(1)} %fusion.90) | copy-start | bytes 49156
  60.5 20.2 %all-to-all-start.1 = ((bf16[8,128,512]{1,2,0:T(8,128)(2,1)}), bf16[8,128,512]{1,2,0:T(8,128)(2,1)}, u32[]{:S(2)}, u32[]{:S(2)}) async-start(bf16[8,128,512]{1,2,0:T(8,128)(2,1)} %bitcast_dynamic-update-slice_fusion.2), calls=%async_computation.1 | async-start | bytes 2097152 | tf_op jit(solution)/shard_map/all_to_all | solution.py:168
  80.8 21.5 %all-to-all-start.5 = ((bf16[128,8,512]{0,2,1:T(8,128)(2,1)}), bf16[128,8,512]{0,2,1:T(8,128)(2,1)S(1)}, u32[]{:S(2)}, u32[]{:S(2)}) async-start(bf16[128,8,512]{0,2,1:T(8,128)(2,1)} %bitcast.368), calls=%async_computation.5 | async-start | bytes 2097152 | tf_op jit(solution)/shard_map/all_to_all | solution.py:164
  85.1 57.0 %all-gather.14.cloned.1.call-start = ((), (), s32[]{:S(2)}) async-start(), calls=%async_computation.10 | async-start | bytes 2359296 | tf_op jit(solution)/shard_map/all_gather | solution.py:23
  101.5 0.7 copy-start.1
  102.3 81.2 %all-gather.16.cloned.1.call-start = ((), (), s32[]{:S(2)}) async-start(), calls=%async_computation.11 | async-start | bytes 2359296 | tf_op jit(solution)/shard_map/all_gather | solution.py:23
  102.3 2.5 copy-start.5
  108.5 10.1 %copy-start.14 = (u32[256]{0:T(256)S(1)}, u32[256]{0:T(256)}, u32[]{:S(2)}) copy-start(u32[256]{0:T(256)} %constant.92) | copy-start | bytes 3076
  117.7 0.7 copy-start
  118.5 95.3 %all-gather.10.cloned.1.call-start = ((), (), s32[]{:S(2)}) async-start(), calls=%async_computation.8 | async-start | bytes 1310720 | tf_op jit(solution)/shard_map/all_gather | solution.py:23
  144.6 97.7 %all-gather.12.cloned.1.call-start = ((), (), s32[]{:S(2)}) async-start(), calls=%async_computation.9 | async-start | bytes 1310720 | tf_op jit(solution)/shard_map/all_gather | solution.py:23
  213.7 2.5 copy-start.4
  216.2 1.9 copy-start.7
  221.1 27.1 %all-to-all-start.4 = ((bf16[8,128,512]{1,2,0:T(8,128)(2,1)}), bf16[8,128,512]{1,2,0:T(8,128)(2,1)}, u32[]{:S(2)}, u32[]{:S(2)}) async-start(bf16[8,128,512]{1,2,0:T(8,128)(2,1)} %bitcast.371), calls=%async_computation.4 | async-start | bytes 2097152 | tf_op jit(solution)/shard_map/all_to_all | solution.py:203
  242.3 2.3 copy-start.3
  245.2 1.2 copy-start.6
  245.2 1.5 copy-start.9
  248.2 21.1 %all-to-all-start.6 = ((bf16[8,128,512]{1,2,0:T(8,128)(2,1)}), bf16[8,128,512]{1,2,0:T(8,128)(2,1)}, u32[]{:S(2)}, u32[]{:S(2)}) async-start(bf16[8,128,512]{1,2,0:T(8,128)(2,1)} %bitcast.367), calls=%async_computation.6 | async-start | bytes 2097152 | tf_op jit(solution)/shard_map/all_to_all | solution.py:204
  258.1 1.6 copy-start.10
  269.3 19.4 %all-to-all-start.7 = ((bf16[8,128,512]{1,2,0:T(8,128)(2,1)}), bf16[8,128,512]{1,2,0:T(8,128)(2,1)S(1)}, u32[]{:S(2)}, u32[]{:S(2)}) async-start(bf16[8,128,512]{1,2,0:T(8,128)(2,1)} %bitcast.372), calls=%async_computation.7 | async-start | bytes 2097152 | tf_op jit(solution)/shard_map/all_to_all | solution.py:205
Sparse Core Ops, SparseCore 0:
  102.4 39.6 all-gather.13
  143.9 39.5 all-gather.15
  185.9 27.8 all-gather.9
  215.4 26.8 all-gather.11
